TPU v7x, 128 devices: a whole 4x4x4 slice. The times are simulated.
128 devices in a mesh: dp: 32 (over z_hi, x, y), mp: 4 (over z_lo, core).
Axes of the slice: x: 4, y: 4, z: 4 (z_hi: 2, z_lo: 2; z = z_hi * 2 + z_lo), core: 2. Of those that a mesh axis runs over, the one named last changes fastest.
Arguments:
- sample_grad: bfloat16 [4608, 8192], P('dp', 'mp'), may hold values from -3 to 3
- advantage: int32 [4608], P('dp'), may hold values from 1024 to 8191
- route_rows: int32 [32, 144], P('dp'), may hold values from 0 to 143, each once within a row
- route_count: int32 [32, 32], P('dp'), may hold values from 1 to 4, 80 in all within a row
- gate_pre: bfloat16 [4096, 16384], P('mp', 'dp'), may hold values from -5 to 5
- up_pre: bfloat16 [4096, 16384], P('mp', 'dp'), may hold values from -5 to 5
- down_weight: bfloat16 [16384, 8192], P('dp', 'mp'), may hold values from -0.046875 to 0.046875
Outputs:
- grad_down: float32 [16384, 8192], P('dp', 'mp')
- grad_gate: bfloat16 [4096, 16384], P('mp', 'dp')
- grad_up: bfloat16 [4096, 16384], P('mp', 'dp')
Inputs may be any that keep to these rules, and one draw needn't show every extreme that they name: Each row of route_rows is a permutation of the sampler's 144 row numbers. `route_count`: each sampler sends every learner at least one row and 80 rows in all; in each sampler's row some learner receives exactly 4.
All inputs are finite; a program needn't handle non-finite values.
Results may differ from a plain program's by a relative error of at most 0.005.
Values may be sent and summed in bfloat16 or wider, within the bound.
No kernel may reach another device: no remote copies, remote signals or barrier semaphores. Data moves between devices by JAX's collectives and lax.ppermute only.
A program may use at most 128 MiB of HBM per device.

v0:
```python
import jax
import jax.numpy as jnp
from jax import lax
from jax.sharding import PartitionSpec as P

SLOTS = 128
LIVE = SLOTS * 5 // 8


def silu_parts(gate_in):
    sigmoid_val = jax.nn.sigmoid(gate_in)
    return (gate_in * sigmoid_val, sigmoid_val * (1.0 + gate_in * (1.0 - sigmoid_val)))


def mp_gather(hidden):
    n_mp = lax.axis_size("mp")
    half = n_mp // 2
    me = lax.axis_index("mp")
    far = lax.ppermute(hidden, "mp", [(i, (i + half) % n_mp) for i in range(n_mp)])
    pair = jnp.stack([hidden, far])
    near = lax.ppermute(pair, "mp", [(i, i ^ 1) for i in range(n_mp)])
    held = jnp.concatenate([pair, near])
    block = jnp.arange(n_mp, dtype=jnp.int32)
    where = jnp.where((block ^ me) % half == 0, 0, 1) * 2 + jnp.where(block ^ me >= half, 1, 0)
    return jnp.take(held, where, axis=0, mode="clip").reshape(
        n_mp * hidden.shape[0], hidden.shape[1]
    )


def dp_gather_small(block):
    n = lax.axis_size("dp")
    me = lax.axis_index("dp")
    held = block
    step = 1
    while step < n:
        theirs = lax.ppermute(held, "dp", [(i, i ^ step) for i in range(n)])
        low = me & step == 0
        held = jnp.where(low, jnp.concatenate([held, theirs]), jnp.concatenate([theirs, held]))
        step *= 2
    return held


def shards(sample_grad, advantage, route_rows, route_count, gate_pre, up_pre, down_weight):
    learners = lax.axis_size("dp")
    capacity = SLOTS // learners
    own = route_count[0]
    own_end = jnp.cumsum(own)
    pos = jnp.arange(LIVE, dtype=jnp.int32)
    before = own_end[None, :] <= pos[:, None]
    own_m = jnp.sum(before.astype(jnp.int32), axis=1)
    own_c = pos - jnp.sum(jnp.where(before, own[None, :], 0), axis=1)
    picked = route_rows[0][own_m * capacity + own_c]
    weights = advantage.astype(jnp.float32) * (1.0 / 4096.0)
    scaled = (sample_grad[picked].astype(jnp.float32) * weights[picked][:, None]).astype(
        jnp.bfloat16
    )
    sent, gate_late, up_late, own_late = lax.optimization_barrier(
        (scaled, gate_pre, up_pre, route_count)
    )
    gate_in = gate_late.astype(jnp.float32)
    up_in = up_late.astype(jnp.float32)
    activated, slopes = silu_parts(gate_in)
    hidden = (activated * up_in).astype(jnp.bfloat16)
    gathered = lax.all_gather(sent, "dp", axis=0, tiled=True)
    hidden_all = mp_gather(hidden)
    counts = dp_gather_small(own_late)
    everything = gathered
    ends = jnp.cumsum(counts, axis=1)
    starts = ends - counts
    done = ends[:, None, :] <= pos[None, :, None]
    m_of = jnp.sum(done.astype(jnp.int32), axis=2)
    c_of = pos[None, :] - jnp.sum(jnp.where(done, counts[:, None, :], 0), axis=2)
    sender = jnp.arange(learners, dtype=jnp.int32)[:, None]
    slot_of = (m_of * SLOTS + sender * capacity + c_of).reshape(-1)
    hidden_live = hidden_all[slot_of]
    everything, hidden_live = lax.optimization_barrier((everything, hidden_live))
    partial_live = lax.dot_general(
        everything, down_weight, (((1,), (1,)), ((), ())), preferred_element_type=jnp.float32
    )
    lane = jnp.arange(capacity, dtype=jnp.int32)
    live = (lane[None, None, :] < counts.T[:, :, None]).reshape(-1)
    first = jnp.arange(learners, dtype=jnp.int32)[None, :] * LIVE + starts.T
    source = jnp.where(live, (first[:, :, None] + lane[None, None, :]).reshape(-1), 0)
    me = lax.axis_index("mp")
    n_mp = lax.axis_size("mp")
    rows_per = hidden.shape[0]

    def partial_block(partial, b):
        return partial[lax.dynamic_slice_in_dim(source, b * rows_per, rows_per)]

    pairs_core = [(i, i ^ 1) for i in range(n_mp)]
    from_core = lax.ppermute(partial_block(partial_live, me ^ 3), "mp", pairs_core)
    to_chip = (partial_block(partial_live, me ^ 2) + from_core).astype(jnp.bfloat16)
    to_chip, partial_late = lax.optimization_barrier((to_chip, partial_live))
    from_chip = lax.ppermute(to_chip, "mp", [(i, i ^ 2) for i in range(n_mp)])
    from_core_own = lax.ppermute(partial_block(partial_late, me ^ 1), "mp", pairs_core)
    own_part = partial_block(partial_late, me)
    grad_down = lax.dot_general(
        hidden_live, everything, (((0,), (0,)), ((), ())), preferred_element_type=jnp.float32
    )
    hidden_grad = own_part + from_core_own + from_chip.astype(jnp.float32)
    hidden_grad = jnp.where(
        lax.dynamic_slice_in_dim(live, me * rows_per, rows_per)[:, None], hidden_grad, 0.0
    )
    grad_gate = (hidden_grad * up_in * slopes).astype(jnp.bfloat16)
    grad_up = (hidden_grad * activated).astype(jnp.bfloat16)
    return (grad_down, grad_gate, grad_up)


def solution(mesh):
    placed = (
        P("dp", "mp"),
        P("dp"),
        P("dp", None),
        P("dp", None),
        P("mp", "dp"),
        P("mp", "dp"),
        P("dp", "mp"),
    )
    return jax.shard_map(
        shards,
        mesh=mesh,
        in_specs=placed,
        out_specs=(P("dp", "mp"), P("mp", "dp"), P("mp", "dp")),
        check_vma=False,
    )
```

profile of v0, /device:TPU:1, one launch (start us, length us, event | category | flops | bytes accessed | tf_op | source)
XLA Modules:
  0.0 209.8 jit_solution(445629079293870821)
XLA Ops:
  7.2 0.0 copy-start
  7.2 0.0 copy-start.1
  7.2 0.0 all-gather.2.cloned.1.call-start
  7.2 0.9 convert_multiply_fusion.4
  8.1 0.7 copy.16
  8.8 0.1 reduce-window.8
  8.9 0.1 reduce
  9.0 0.7 convert_reduce_fusion.1
  9.8 1.6 gather_fusion
  11.4 1.3 gather_fusion.2
  12.7 0.0 copy-done.1
  12.7 0.8 gather_fusion.1
  13.5 0.0 copy-start.4
  13.5 0.8 multiply_convert_fusion.1
  14.4 0.0 all-gather.2.cloned.1.call-update
  14.4 2.2 %fusion = bf16[1024,512]{1,0:T(8,128)(2,1)S(1)} fusion(bf16[1024,512]{1,0:T(8,128)(2,1)} %param.12, bf16[1024,512]{1,0:T(8,128)(2,1)} %param.11), kind=kLoop, calls=%fused_computation.15 | loop fusion | flops 4194304 | bytes 3145728 | tf_op jit(solution)/shard_map/convert_element_type | solution.py:63
  16.6 2.5 %collective-permute-start = (bf16[1024,512]{1,0:T(8,128)(2,1)S(1)}, bf16[1024,512]{1,0:T(8,128)(2,1)}, u32[]{:S(2)}, u32[]{:S(2)}) collective-permute-start(bf16[1024,512]{1,0:T(8,128)(2,1)S(1)} %fusion), channel_id=1, source_target_pairs={{0,2},{1,3},{2,0},{3,1},{4,6},{5,7},{6,4},{7,5},{8,10},{9,11},{10,... | collective-permute-start | bytes 3145736 | tf_op jit(solution)/shard_map/ppermute | solution.py:19
  19.1 0.0 copy-done.4
  19.1 1.3 collective-permute-start.2
  20.5 1.5 collective-permute-done.2
  22.0 3.0 %collective-permute-start.3 = (s32[2,32]{1,0:T(2,128)S(1)}, s32[2,32]{1,0:T(2,128)S(1)}, u32[]{:S(2)}, u32[]{:S(2)}) collective-permute-start(s32[2,32]{1,0:T(2,128)S(1)} %add_select_fusion.5), channel_id=1, source_target_pairs={{0,8},{4,12},{8,0},{12,4},{16,24},{20,28},{24,16},{28,20},{32,40},... | collective-permute-start | bytes 776 | tf_op jit(solution)/shard_map/ppermute | solution.py:36
  25.0 1.0 collective-permute-done.3
  26.0 1.3 collective-permute-start.4
  27.3 17.2 %collective-permute-done = bf16[1024,512]{1,0:T(8,128)(2,1)} collective-permute-done((bf16[1024,512]{1,0:T(8,128)(2,1)S(1)}, bf16[1024,512]{1,0:T(8,128)(2,1)}, u32[]{:S(2)}, u32[]{:S(2)}) %collective-permute-start) | collective-permute-done | bytes 1048608 | tf_op jit(solution)/shard_map/ppermute | solution.py:19
  44.4 2.7 %pad_maximum_fusion.1 = bf16[2,1024,512]{2,1,0:T(8,128)(2,1)} fusion(bf16[1,1024,512]{2,1,0:T(8,128)(2,1)} %bitcast.9, bf16[1,1024,512]{2,1,0:T(8,128)(2,1)S(1)} %bitcast.31), kind=kLoop, calls=%fused_computation.23 | loop fusion | flops 1048576 | bytes 4194304 | tf_op jit(solution)/shard_map/stack | solution.py:20
  47.2 1.3 collective-permute-start.1
  48.4 0.0 collective-permute-done.4
  48.4 2.8 %collective-permute-start.5 = (s32[8,32]{1,0:T(8,128)S(1)}, s32[8,32]{1,0:T(8,128)S(1)}, u32[]{:S(2)}, u32[]{:S(2)}) collective-permute-start(s32[8,32]{1,0:T(8,128)S(1)} %add_select_fusion.3), channel_id=1, source_target_pairs={{0,32},{4,36},{8,40},{12,44},{16,48},{20,52},{24,56},{28,60},{32,0... | collective-permute-start | bytes 3080 | tf_op jit(solution)/shard_map/ppermute | solution.py:36
  51.3 1.2 collective-permute-done.5
  52.5 3.4 %collective-permute-start.6 = (s32[16,32]{1,0:T(8,128)S(1)}, s32[16,32]{1,0:T(8,128)S(1)}, u32[]{:S(2)}, u32[]{:S(2)}) collective-permute-start(s32[16,32]{1,0:T(8,128)S(1)} %add_select_fusion.2), channel_id=1, source_target_pairs={{0,64},{4,68},{8,72},{12,76},{16,80},{20,84},{24,88},{28,92},{32,9... | collective-permute-start | bytes 6152 | tf_op jit(solution)/shard_map/ppermute | solution.py:36
  55.9 1.7 collective-permute-done.6
  57.6 0.2 reduce_window_sum.18
  57.8 0.1 add_bitcast_fusion
  57.9 0.1 copy.18
  58.0 0.1 copy.17
  58.0 0.4 convert_reduce_fusion
  58.4 0.1 subtract_add_fusion
  58.5 0.1 add.173
  58.6 0.2 iota_compare_fusion
  58.8 0.3 lt.92
  59.2 1.0 iota_add_fusion
  60.1 1.3 add.182
  61.6 0.0 collective-permute-done.1
  61.6 3.6 %pad_maximum_fusion = bf16[4,1024,512]{2,1,0:T(8,128)(2,1)} fusion(bf16[2,1024,512]{2,1,0:T(8,128)(2,1)} %collective-permute-done.1, bf16[1,1024,512]{2,1,0:T(8,128)(2,1)} %bitcast.9, bf16[1,1024,512]{2,1,0:T(8,128)(2,1)S(1)} %bitcast.32), kind=kLoop, calls=%fused_computation.9 | loop fusion | flops 4194304 | bytes 8388608 | tf_op jit(solution)/shard_map/concatenate | solution.py:22
  65.2 5.1 %gather_fusion.3 = bf16[4,1024,512]{2,1,0:T(8,128)(2,1)} fusion(bf16[4,1024,512]{2,1,0:T(8,128)(2,1)} %pad_maximum_fusion, s32[1024]{0:T(1024)S(1)} %pad_clamp_fusion.1), kind=kCustom, calls=%fused_computation.3 | custom fusion | bytes 8388624 | tf_op jit(solution)/shard_map/jit(_take)/gather | solution.py:25
  70.3 11.1 %gather_fusion.4 = bf16[2560,512]{1,0:T(8,128)(2,1)} fusion(bf16[4096,512]{1,0:T(8,128)(2,1)} %bitcast.30, s32[3072]{0:T(1024)S(1)} %pad_clamp_fusion), kind=kCustom, calls=%fused_computation.4 | custom fusion | bytes 5253120 | tf_op jit(solution)/shard_map/gather | solution.py:75
  81.4 54.4 %all-gather.2.cloned.1.call-done = bf16[2560,2048]{1,0:T(8,128)(2,1)} async-done(((bf16[80,2048]{1,0:T(8,128)(2,1)}), bf16[2560,2048]{1,0:T(8,128)(2,1)}) %all-gather.2.cloned.1.call-update) | async-done | bytes 10485776 | tf_op jit(solution)/shard_map/all_gather | solution.py:64
  135.7 0.0 copy-done
  135.7 9.8 %fusion.21 = f32[2560,512]{1,0:T(8,128)} fusion(bf16[2560,2048]{1,0:T(8,128)(2,1)} %all-gather.2.cloned.1.call-done, bf16[512,2048]{1,0:T(8,128)(2,1)S(1)} %copy-done), kind=kOutput, calls=%fused_computation.77 | convolution fusion | flops 5368709120 | bytes 17825792 | tf_op jit(solution)/shard_map/dot_general | solution.py:77
  145.6 7.8 %gather_fusion.6 = f32[1024,512]{1,0:T(8,128)} fusion(f32[2560,512]{1,0:T(8,128)} %fusion.21, s32[1024]{0:T(1024)S(1)} %get-tuple-element.27), kind=kCustom, calls=%fused_computation.6 | custom fusion | bytes 4198400 | tf_op jit(solution)/shard_map/gather | solution.py:89
  153.4 1.4 collective-permute-start.7
  154.8 7.8 %gather_fusion.5 = f32[1024,512]{1,0:T(8,128)} fusion(f32[2560,512]{1,0:T(8,128)} %fusion.21, s32[1024]{0:T(1024)S(1)} %get-tuple-element.28), kind=kCustom, calls=%fused_computation.5 | custom fusion | bytes 4198400 | tf_op jit(solution)/shard_map/gather | solution.py:89
  162.5 0.0 collective-permute-done.7
  162.5 3.5 %add_convert_fusion = bf16[1024,512]{1,0:T(8,128)(2,1)} fusion(f32[1024,512]{1,0:T(8,128)} %gather_fusion.5, f32[1024,512]{1,0:T(8,128)} %collective-permute-done.7), kind=kLoop, calls=%fused_computation.26 | loop fusion | flops 1048576 | bytes 5242880 | tf_op jit(solution)/shard_map/convert_element_type | solution.py:93
  166.1 7.8 %gather_fusion.8 = f32[1024,512]{1,0:T(8,128)} fusion(f32[2560,512]{1,0:T(8,128)} %fusion.21, s32[1024]{0:T(1024)S(1)} %get-tuple-element.25), kind=kCustom, calls=%fused_computation.8 | custom fusion | bytes 4198400 | tf_op jit(solution)/shard_map/gather | solution.py:89
  173.8 0.0 collective-permute-start.8
  173.8 0.0 copy-done.3
  173.8 0.4 collective-permute-start.9
  174.2 10.4 %fusion.20 = f32[512,2048]{1,0:T(8,128)} fusion(bf16[2560,512]{1,0:T(8,128)(2,1)} %gather_fusion.4, bf16[2560,2048]{1,0:T(8,128)(2,1)} %all-gather.2.cloned.1.call-done), kind=kOutput, calls=%fused_computation.76 | convolution fusion | flops 5368709120 | bytes 17301504 | tf_op jit(solution)/shard_map/dot_general | solution.py:98
  184.6 7.9 %gather_fusion.7 = f32[1024,512]{1,0:T(8,128)} fusion(f32[2560,512]{1,0:T(8,128)} %fusion.21, s32[1024]{0:T(1024)S(1)} %get-tuple-element.26), kind=kCustom, calls=%fused_computation.7 | custom fusion | bytes 4198400 | tf_op jit(solution)/shard_map/gather | solution.py:89
  192.5 5.9 %collective-permute-done.9 = bf16[1024,512]{1,0:T(8,128)(2,1)} collective-permute-done((bf16[1024,512]{1,0:T(8,128)(2,1)}, bf16[1024,512]{1,0:T(8,128)(2,1)}, u32[]{:S(2)}, u32[]{:S(2)}) %collective-permute-start.9) | collective-permute-done | bytes 1048608 | tf_op jit(solution)/shard_map/ppermute | solution.py:95
  198.4 0.0 collective-permute-done.8
  198.4 0.0 copy-done.2
  198.4 4.6 %multiply_convert_fusion = (bf16[1024,512]{1,0:T(8,128)(2,1)}, bf16[1024,512]{1,0:T(8,128)(2,1)}) fusion(bf16[1024,512]{1,0:T(8,128)(2,1)} %param.11, bf16[1024,512]{1,0:T(8,128)(2,1)} %collective-permute-done.9, f32[1024,512]{1,0:T(8,128)} %gather_fusion.7, f32[1024,512]{1,0:T(8,128)} %collective-permute-done.8, pred[1024]{0:T(1024)(128)(4,1)S(1)} %dynamic-slice-done, ...), kind=kLoop, calls=%fused_computation.24 | loop fusion | flops 9961472 | bytes 9438208 | tf_op jit(solution)/shard_map/convert_element_type | solution.py:106
  (21 shorter events, 0.2 us)
Async XLA Ops:
  7.2 128.6 %copy-start = (bf16[512,2048]{1,0:T(8,128)(2,1)S(1)}, bf16[512,2048]{1,0:T(8,128)(2,1)}, u32[]{:S(2)}) copy-start(bf16[512,2048]{1,0:T(8,128)(2,1)} %param.13) | copy-start | bytes 6291460
  7.2 5.5 %copy-start.1 = (bf16[144,2048]{1,0:T(8,128)(2,1)S(1)}, bf16[144,2048]{1,0:T(8,128)(2,1)}, u32[]{:S(2)}) copy-start(bf16[144,2048]{1,0:T(8,128)(2,1)} %param.7) | copy-start | bytes 1769476
  7.2 128.5 %all-gather.2.cloned.1.call-start = ((), (), s32[]{:S(2)}) async-start(), calls=%async_computation | async-start | bytes 10813440 | tf_op jit(solution)/shard_map/all_gather | solution.py:64
  13.5 5.6 %copy-start.4 = (s32[1,32]{1,0:T(1,128)S(1)}, s32[1,32]{1,0:T(1,128)}, u32[]{:S(2)}) copy-start(s32[1,32]{1,0:T(1,128)} %param.10) | copy-start | bytes 388
  16.6 27.8 %collective-permute-start = (bf16[1024,512]{1,0:T(8,128)(2,1)S(1)}, bf16[1024,512]{1,0:T(8,128)(2,1)}, u32[]{:S(2)}, u32[]{:S(2)}) collective-permute-start(bf16[1024,512]{1,0:T(8,128)(2,1)S(1)} %fusion), channel_id=1, source_target_pairs={{0,2},{1,3},{2,0},{3,1},{4,6},{5,7},{6,4},{7,5},{8,10},{9,11},{10,... | collective-permute-start | bytes 3145736 | tf_op jit(solution)/shard_map/ppermute | solution.py:19
  19.1 2.8 %collective-permute-start.2 = (s32[1,32]{1,0:T(1,128)S(1)}, s32[1,32]{1,0:T(1,128)S(1)}, u32[]{:S(2)}, u32[]{:S(2)}) collective-permute-start(s32[1,32]{1,0:T(1,128)S(1)} %copy-done.4), channel_id=1, source_target_pairs={{0,4},{4,0},{8,12},{12,8},{16,20},{20,16},{24,28},{28,24},{32,36},... | collective-permute-start | bytes 392 | tf_op jit(solution)/shard_map/ppermute | solution.py:36
  22.0 4.0 %collective-permute-start.3 = (s32[2,32]{1,0:T(2,128)S(1)}, s32[2,32]{1,0:T(2,128)S(1)}, u32[]{:S(2)}, u32[]{:S(2)}) collective-permute-start(s32[2,32]{1,0:T(2,128)S(1)} %add_select_fusion.5), channel_id=1, source_target_pairs={{0,8},{4,12},{8,0},{12,4},{16,24},{20,28},{24,16},{28,20},{32,40},... | collective-permute-start | bytes 776 | tf_op jit(solution)/shard_map/ppermute | solution.py:36
  26.0 22.4 %collective-permute-start.4 = (s32[4,32]{1,0:T(4,128)S(1)}, s32[4,32]{1,0:T(4,128)S(1)}, u32[]{:S(2)}, u32[]{:S(2)}) collective-permute-start(s32[4,32]{1,0:T(4,128)S(1)} %add_select_fusion.4), channel_id=1, source_target_pairs={{0,16},{4,20},{8,24},{12,28},{16,0},{20,4},{24,8},{28,12},{32,48},... | collective-permute-start | bytes 1544 | tf_op jit(solution)/shard_map/ppermute | solution.py:36
  47.2 14.4 %collective-permute-start.1 = (bf16[2,1024,512]{2,1,0:T(8,128)(2,1)}, bf16[2,1024,512]{2,1,0:T(8,128)(2,1)}, u32[]{:S(2)}, u32[]{:S(2)}) collective-permute-start(bf16[2,1024,512]{2,1,0:T(8,128)(2,1)} %pad_maximum_fusion.1), channel_id=1, source_target_pairs={{0,1},{1,0},{2,3},{3,2},{4,5},{5,4},{6,7},{7,6},{8,9},{9,8},{10,11... | collective-permute-start | bytes 6291464 | tf_op jit(solution)/shard_map/ppermute | solution.py:21
  48.4 4.0 %collective-permute-start.5 = (s32[8,32]{1,0:T(8,128)S(1)}, s32[8,32]{1,0:T(8,128)S(1)}, u32[]{:S(2)}, u32[]{:S(2)}) collective-permute-start(s32[8,32]{1,0:T(8,128)S(1)} %add_select_fusion.3), channel_id=1, source_target_pairs={{0,32},{4,36},{8,40},{12,44},{16,48},{20,52},{24,56},{28,60},{32,0... | collective-permute-start | bytes 3080 | tf_op jit(solution)/shard_map/ppermute | solution.py:36
  52.5 5.2 %collective-permute-start.6 = (s32[16,32]{1,0:T(8,128)S(1)}, s32[16,32]{1,0:T(8,128)S(1)}, u32[]{:S(2)}, u32[]{:S(2)}) collective-permute-start(s32[16,32]{1,0:T(8,128)S(1)} %add_select_fusion.2), channel_id=1, source_target_pairs={{0,64},{4,68},{8,72},{12,76},{16,80},{20,84},{24,88},{28,92},{32,9... | collective-permute-start | bytes 6152 | tf_op jit(solution)/shard_map/ppermute | solution.py:36
  59.1 114.7 %copy-start.3 = (pred[4096]{0:T(1024)(128)(4,1)}, pred[4096]{0:T(1024)(128)(4,1)S(1)}, u32[]{:S(2)}) copy-start(pred[4096]{0:T(1024)(128)(4,1)S(1)} %lt.92) | copy-start | bytes 12292
  153.4 9.2 %collective-permute-start.7 = (f32[1024,512]{1,0:T(8,128)}, f32[1024,512]{1,0:T(8,128)}, u32[]{:S(2)}, u32[]{:S(2)}) collective-permute-start(f32[1024,512]{1,0:T(8,128)} %gather_fusion.6), channel_id=1, source_target_pairs={{0,1},{1,0},{2,3},{3,2},{4,5},{5,4},{6,7},{7,6},{8,9},{9,8},{10,11... | collective-permute-start | bytes 6291464 | tf_op jit(solution)/shard_map/ppermute | solution.py:92
  173.8 24.5 %collective-permute-start.8 = (f32[1024,512]{1,0:T(8,128)}, f32[1024,512]{1,0:T(8,128)}, u32[]{:S(2)}, u32[]{:S(2)}) collective-permute-start(f32[1024,512]{1,0:T(8,128)} %gather_fusion.8), channel_id=1, source_target_pairs={{0,1},{1,0},{2,3},{3,2},{4,5},{5,4},{6,7},{7,6},{8,9},{9,8},{10,11... | collective-permute-start | bytes 6291464 | tf_op jit(solution)/shard_map/ppermute | solution.py:96
  173.8 24.5 %collective-permute-start.9 = (bf16[1024,512]{1,0:T(8,128)(2,1)}, bf16[1024,512]{1,0:T(8,128)(2,1)}, u32[]{:S(2)}, u32[]{:S(2)}) collective-permute-start(bf16[1024,512]{1,0:T(8,128)(2,1)} %add_convert_fusion), channel_id=1, source_target_pairs={{0,2},{1,3},{2,0},{3,1},{4,6},{5,7},{6,4},{7,5},{8,10},{9,11},{10,... | collective-permute-start | bytes 3145736 | tf_op jit(solution)/shard_map/ppermute | solution.py:95
  184.6 13.7 %copy-start.2 = (bf16[1024,512]{1,0:T(8,128)(2,1)S(1)}, bf16[1024,512]{1,0:T(8,128)(2,1)}, u32[]{:S(2)}) copy-start(bf16[1024,512]{1,0:T(8,128)(2,1)} %param.12) | copy-start | bytes 3145732
  184.6 13.7 %dynamic-slice-start = ((pred[4096]{0:T(1024)(128)(4,1)}, s32[]{:T(128)}), pred[1024]{0:T(1024)(128)(4,1)S(1)}, s32[]{:S(2)}) async-start(pred[4096]{0:T(1024)(128)(4,1)} %copy-done.3, s32[]{:T(128)} %select_n.172), calls=%async_computation.1 | async-start | bytes 2560 | tf_op jit(solution)/shard_map/dynamic_slice | solution.py:103
Sparse Core Ops, SparseCore 0:
  14.5 121.1 all-gather.1
where the time goes:
time: 210 us
  waiting for transfers between devices  82.9 us (39%)
  local copies, waits for them, and re-layouts  53.7 us (26%)
  other arithmetic  21.4 us (10%)
  matrix products  20.2 us (10%)
  starting transfers between devices  17.4 us (8%)
  between operations  14.2 us (7%)
    all_gather x1, waiting for transfers between devices, shards(): gathered = lax.all_gather(sent, 'dp', axis=0, tiled=True)  54.4 us
    gather x4, local copies, waits for them, and re-layouts, partial_block(): return partial[lax.dynamic_slice_in_dim(source, b * rows_per, rows_per)]  31.2 us
    ppermute x1, waiting for transfers between devices, mp_gather(): lax.ppermute(hidden, 'mp', [(i, (i + half) % n_mp) for i in range(n_mp)])  17.2 us
    ppermute x5, starting transfers between devices, dp_gather_small(): theirs = lax.ppermute(held, 'dp', [(i, i ^ step) for i in range(n)])  11.8 us
    gather x1, local copies, waits for them, and re-layouts, shards(): hidden_live = hidden_all[slot_of]  11.1 us
    dot_general x1, matrix products, shards(): lax.dot_general(hidden_live, everything, (((0,), (0,)), ((), ())), prefer...  10.4 us
    dot_general x1, matrix products, shards(): lax.dot_general(everything, down_weight, (((1,), (1,)), ((), ())), prefer...  9.82 us
    ppermute x1, waiting for transfers between devices, shards(): from_chip = lax.ppermute(to_chip, 'mp', [(i, i ^ 2) for i in range(n_mp)])  5.87 us
  transfers between devices with their start and end apart: 11, of which 7 were waited for; matrix products, arithmetic and copies ran while one was open for 26% of the time, Pallas kernels for 0%

commit v1 on v0

--- a/solution.py
+++ b/solution.py
@@ -1,10 +1,21 @@
+import functools
 import jax
 import jax.numpy as jnp
 from jax import lax
 from jax.sharding import PartitionSpec as P
+from jax.lax import all_to_all, axis_size
 
 SLOTS = 128
 LIVE = SLOTS * 5 // 8
+
+
+def play_the_lots_all(sample, named_axis, dim_i):
+    state_next = jnp.stack([sample] * axis_size(named_axis), 0)
+    tile_out = all_to_all(state_next, named_axis, 0, 0)
+    return jnp.concatenate(tile_out, dim_i)
+
+
+_time_fields = functools.partial(play_the_lots_all, named_axis="dp", dim_i=0)
 
 
 def silu_parts(gate_in):
@@ -61,7 +72,7 @@
     up_in = up_late.astype(jnp.float32)
     activated, slopes = silu_parts(gate_in)
     hidden = (activated * up_in).astype(jnp.bfloat16)
-    gathered = lax.all_gather(sent, "dp", axis=0, tiled=True)
+    gathered = _time_fields(sent)
     hidden_all = mp_gather(hidden)
     counts = dp_gather_small(own_late)
     everything = gathered

time: 210 us -> 286 us (1.36); the launches traced: 210 us -> 280 us
  waiting for transfers between devices: 82.9 us -> 136 us
  starting transfers between devices: 17.4 us -> 46.6 us
  between operations: 14.2 us -> 0.94 us
    ppermute x5, waiting for transfers between devices: 5.46 us -> 117 us  [dp_gather_small(): theirs = lax.ppermute(held, 'dp', [(i, i ^ step) for i in range(n)])]
    all_gather x1 -> x0, waiting for transfers between devices: 54.4 us -> none  [shards(): gathered = lax.all_gather(sent, 'dp', axis=0, tiled=True)]
    ppermute x5, starting transfers between devices: 11.8 us -> 28 us  [dp_gather_small(): theirs = lax.ppermute(held, 'dp', [(i, i ^ step) for i in range(n)])]
    all_to_all x0 -> x1, starting transfers between devices: none -> 11.3 us  [play_the_lots_all(): tile_out = all_to_all(state_next, named_axis, 0, 0)]
    another operation x1 -> x2, local copies, waits for them, and re-layouts: 0.74 us -> 6.06 us  [the longest x1 5.16 us: play_the_lots_all(): state_next = jnp.stack([sample] * axis_size(named_axis), 0)]
    ppermute x1, waiting for transfers between devices: 17.2 us -> 13.2 us  [mp_gather(): lax.ppermute(hidden, 'mp', [(i, (i + half) % n_mp) for i in range(n_mp)])]
  transfers between devices with their start and end apart: 11 -> 11, of which waited for: 7 -> 7; matrix products, arithmetic and copies ran while one was open for 26% -> 19% of each run, Pallas kernels for 0% -> 0%
where the time goes in v1:
time: 286 us; the launch traced here: 280 us
  waiting for transfers between devices  136 us (48%)
  local copies, waits for them, and re-layouts  56.3 us (20%)
  starting transfers between devices  46.6 us (16%)
  matrix products  20.2 us (7%)
  other arithmetic  20 us (7%)
    ppermute x5, waiting for transfers between devices, dp_gather_small(): theirs = lax.ppermute(held, 'dp', [(i, i ^ step) for i in range(n)])  117 us
    gather x4, local copies, waits for them, and re-layouts, partial_block(): return partial[lax.dynamic_slice_in_dim(source, b * rows_per, rows_per)]  28.6 us
    ppermute x5, starting transfers between devices, dp_gather_small(): theirs = lax.ppermute(held, 'dp', [(i, i ^ step) for i in range(n)])  28 us
    ppermute x1, waiting for transfers between devices, mp_gather(): lax.ppermute(hidden, 'mp', [(i, (i + half) % n_mp) for i in range(n_mp)])  13.2 us
    all_to_all x1, starting transfers between devices, play_the_lots_all(): tile_out = all_to_all(state_next, named_axis, 0, 0)  11.3 us
    gather x1, local copies, waits for them, and re-layouts, shards(): hidden_live = hidden_all[slot_of]  11.1 us
    dot_general x1, matrix products, shards(): lax.dot_general(hidden_live, everything, (((0,), (0,)), ((), ())), prefer...  10.4 us
    dot_general x1, matrix products, shards(): lax.dot_general(everything, down_weight, (((1,), (1,)), ((), ())), prefer...  9.82 us
  transfers between devices with their start and end apart: 11, of which 7 were waited for; matrix products, arithmetic and copies ran while one was open for 19% of the time, Pallas kernels for 0%

profile of v1, /device:TPU:1, one launch (start us, length us, event | category | flops | bytes accessed | tf_op | source)
XLA Modules:
  0.0 280.4 jit_solution(11830865194639356219)
XLA Ops:
  0.6 0.0 copy-start
  0.6 0.0 copy-start.2
  0.7 0.9 copy.16
  1.6 0.1 reduce-window.8
  1.6 0.1 reduce
  1.7 0.7 convert_reduce_fusion.1
  2.5 1.6 gather_fusion
  4.2 0.7 convert_multiply_fusion.4
  4.8 0.0 copy-done.2
  4.8 0.8 gather_fusion.1
  5.6 1.3 gather_fusion.2
  6.9 0.1 multiply_convert_fusion.1
  7.0 5.2 %stack.8 = bf16[32,80,2048]{2,1,0:T(8,128)(2,1)} broadcast(bf16[80,2048]{1,0:T(8,128)(2,1)S(1)} %multiply_convert_fusion.1), dimensions={1,2} | broadcast | bytes 10813440 | tf_op jit(solution)/shard_map/stack | solution.py:13
  12.2 11.3 %all-to-all-start = ((bf16[32,80,2048]{2,1,0:T(8,128)(2,1)}), bf16[32,80,2048]{2,1,0:T(8,128)(2,1)}, u32[]{:S(2)}, u32[]{:S(2)}) async-start(bf16[32,80,2048]{2,1,0:T(8,128)(2,1)} %stack.8), calls=%async_computation | async-start | bytes 20971520 | tf_op jit(solution)/shard_map/all_to_all | solution.py:14
  23.5 0.0 copy-start.5
  23.5 2.2 fusion
  25.7 0.8 collective-permute-start
  26.5 0.0 copy-done.5
  26.5 1.2 collective-permute-start.2
  27.7 92.5 %collective-permute-done.2 = s32[1,32]{1,0:T(1,128)S(1)} collective-permute-done((s32[1,32]{1,0:T(1,128)S(1)}, s32[1,32]{1,0:T(1,128)S(1)}, u32[]{:S(2)}, u32[]{:S(2)}) %collective-permute-start.2) | collective-permute-done | bytes 160 | tf_op jit(solution)/shard_map/ppermute | solution.py:47
  120.3 16.9 %collective-permute-start.3 = (s32[2,32]{1,0:T(2,128)S(1)}, s32[2,32]{1,0:T(2,128)S(1)}, u32[]{:S(2)}, u32[]{:S(2)}) collective-permute-start(s32[2,32]{1,0:T(2,128)S(1)} %add_select_fusion.5), channel_id=1, source_target_pairs={{0,8},{4,12},{8,0},{12,4},{16,24},{20,28},{24,16},{28,20},{32,40},... | collective-permute-start | bytes 776 | tf_op jit(solution)/shard_map/ppermute | solution.py:47
  137.2 1.5 collective-permute-done.3
  138.7 0.1 collective-permute-start.4
  138.8 13.2 %collective-permute-done = bf16[1024,512]{1,0:T(8,128)(2,1)} collective-permute-done((bf16[1024,512]{1,0:T(8,128)(2,1)S(1)}, bf16[1024,512]{1,0:T(8,128)(2,1)}, u32[]{:S(2)}, u32[]{:S(2)}) %collective-permute-start) | collective-permute-done | bytes 1048608 | tf_op jit(solution)/shard_map/ppermute | solution.py:30
  152.0 2.7 pad_maximum_fusion.1
  154.7 1.5 collective-permute-start.1
  156.3 18.5 %collective-permute-done.4 = s32[4,32]{1,0:T(4,128)S(1)} collective-permute-done((s32[4,32]{1,0:T(4,128)S(1)}, s32[4,32]{1,0:T(4,128)S(1)}, u32[]{:S(2)}, u32[]{:S(2)}) %collective-permute-start.4) | collective-permute-done | bytes 544 | tf_op jit(solution)/shard_map/ppermute | solution.py:47
  174.8 9.8 %collective-permute-start.5 = (s32[8,32]{1,0:T(8,128)S(1)}, s32[8,32]{1,0:T(8,128)S(1)}, u32[]{:S(2)}, u32[]{:S(2)}) collective-permute-start(s32[8,32]{1,0:T(8,128)S(1)} %add_select_fusion.3), channel_id=1, source_target_pairs={{0,32},{4,36},{8,40},{12,44},{16,48},{20,52},{24,56},{28,60},{32,0... | collective-permute-start | bytes 3080 | tf_op jit(solution)/shard_map/ppermute | solution.py:47
  184.6 1.0 collective-permute-done.5
  185.6 0.0 collective-permute-start.6
  185.6 4.0 %collective-permute-done.6 = s32[16,32]{1,0:T(8,128)S(1)} collective-permute-done((s32[16,32]{1,0:T(8,128)S(1)}, s32[16,32]{1,0:T(8,128)S(1)}, u32[]{:S(2)}, u32[]{:S(2)}) %collective-permute-start.6) | collective-permute-done | bytes 2080 | tf_op jit(solution)/shard_map/ppermute | solution.py:47
  189.6 0.2 reduce_window_sum.18
  189.8 0.4 convert_reduce_fusion
  190.1 0.1 subtract_add_fusion
  190.2 0.1 add.173
  190.3 0.1 copy.17
  190.4 0.2 iota_compare_fusion
  190.6 0.3 lt.92
  190.9 0.0 copy-start.4
  190.9 0.1 add_bitcast_fusion
  191.0 0.1 copy.18
  191.1 1.0 iota_add_fusion
  192.1 1.3 add.182
  193.5 0.0 collective-permute-done.1
  193.5 3.6 %pad_maximum_fusion = bf16[4,1024,512]{2,1,0:T(8,128)(2,1)} fusion(bf16[2,1024,512]{2,1,0:T(8,128)(2,1)} %collective-permute-done.1, bf16[1,1024,512]{2,1,0:T(8,128)(2,1)} %bitcast.10, bf16[1,1024,512]{2,1,0:T(8,128)(2,1)S(1)} %bitcast.33), kind=kLoop, calls=%fused_computation.9 | loop fusion | flops 4194304 | bytes 8388608 | tf_op jit(solution)/shard_map/concatenate | solution.py:33
  197.1 5.0 %gather_fusion.3 = bf16[4,1024,512]{2,1,0:T(8,128)(2,1)} fusion(bf16[4,1024,512]{2,1,0:T(8,128)(2,1)} %pad_maximum_fusion, s32[1024]{0:T(1024)S(1)} %pad_clamp_fusion.1), kind=kCustom, calls=%fused_computation.3 | custom fusion | bytes 8388624 | tf_op jit(solution)/shard_map/jit(_take)/gather | solution.py:36
  202.0 11.1 %gather_fusion.4 = bf16[2560,512]{1,0:T(8,128)(2,1)} fusion(bf16[4096,512]{1,0:T(8,128)(2,1)} %bitcast.31, s32[3072]{0:T(1024)S(1)} %pad_clamp_fusion), kind=kCustom, calls=%fused_computation.4 | custom fusion | bytes 5253120 | tf_op jit(solution)/shard_map/gather | solution.py:86
  213.1 0.0 all-to-all-done
  213.1 9.8 %fusion.21 = f32[2560,512]{1,0:T(8,128)} fusion(bf16[2560,2048]{1,0:T(8,128)(2,1)} %bitcast.8, bf16[512,2048]{1,0:T(8,128)(2,1)S(1)} %copy-done), kind=kOutput, calls=%fused_computation.77 | convolution fusion | flops 5368709120 | bytes 17825792 | tf_op jit(solution)/shard_map/dot_general | solution.py:88
  223.0 7.8 %gather_fusion.6 = f32[1024,512]{1,0:T(8,128)} fusion(f32[2560,512]{1,0:T(8,128)} %fusion.21, s32[1024]{0:T(1024)S(1)} %get-tuple-element.27), kind=kCustom, calls=%fused_computation.6 | custom fusion | bytes 4198400 | tf_op jit(solution)/shard_map/gather | solution.py:100
  230.7 4.1 %collective-permute-start.7 = (f32[1024,512]{1,0:T(8,128)}, f32[1024,512]{1,0:T(8,128)}, u32[]{:S(2)}, u32[]{:S(2)}) collective-permute-start(f32[1024,512]{1,0:T(8,128)} %gather_fusion.6), channel_id=1, source_target_pairs={{0,1},{1,0},{2,3},{3,2},{4,5},{5,4},{6,7},{7,6},{8,9},{9,8},{10,11... | collective-permute-start | bytes 6291464 | tf_op jit(solution)/shard_map/ppermute | solution.py:103
  234.8 6.5 %gather_fusion.5 = f32[1024,512]{1,0:T(8,128)S(1)} fusion(f32[2560,512]{1,0:T(8,128)} %fusion.21, s32[1024]{0:T(1024)S(1)} %get-tuple-element.28), kind=kCustom, calls=%fused_computation.5 | custom fusion | bytes 4198400 | tf_op jit(solution)/shard_map/gather | solution.py:100
  241.3 0.0 collective-permute-done.7
  241.3 2.9 %add_convert_fusion = bf16[1024,512]{1,0:T(8,128)(2,1)} fusion(f32[1024,512]{1,0:T(8,128)S(1)} %gather_fusion.5, f32[1024,512]{1,0:T(8,128)} %collective-permute-done.7), kind=kLoop, calls=%fused_computation.26 | loop fusion | flops 1048576 | bytes 5242880 | tf_op jit(solution)/shard_map/convert_element_type | solution.py:104
  244.2 6.5 %gather_fusion.8 = f32[1024,512]{1,0:T(8,128)S(1)} fusion(f32[2560,512]{1,0:T(8,128)} %fusion.21, s32[1024]{0:T(1024)S(1)} %get-tuple-element.25), kind=kCustom, calls=%fused_computation.8 | custom fusion | bytes 4198400 | tf_op jit(solution)/shard_map/gather | solution.py:100
  250.7 0.1 collective-permute-start.8
  250.8 0.8 collective-permute-start.9
  251.7 10.4 %fusion.20 = f32[512,2048]{1,0:T(8,128)} fusion(bf16[2560,512]{1,0:T(8,128)(2,1)} %gather_fusion.4, bf16[2560,2048]{1,0:T(8,128)(2,1)} %bitcast.8), kind=kOutput, calls=%fused_computation.76 | convolution fusion | flops 5368709120 | bytes 17301504 | tf_op jit(solution)/shard_map/dot_general | solution.py:109
  262.1 7.9 %gather_fusion.7 = f32[1024,512]{1,0:T(8,128)} fusion(f32[2560,512]{1,0:T(8,128)} %fusion.21, s32[1024]{0:T(1024)S(1)} %get-tuple-element.26), kind=kCustom, calls=%fused_computation.7 | custom fusion | bytes 4198400 | tf_op jit(solution)/shard_map/gather | solution.py:100
  270.0 5.6 %collective-permute-done.9 = bf16[1024,512]{1,0:T(8,128)(2,1)} collective-permute-done((bf16[1024,512]{1,0:T(8,128)(2,1)}, bf16[1024,512]{1,0:T(8,128)(2,1)}, u32[]{:S(2)}, u32[]{:S(2)}) %collective-permute-start.9) | collective-permute-done | bytes 1048608 | tf_op jit(solution)/shard_map/ppermute | solution.py:106
  275.5 0.0 collective-permute-done.8
  275.6 0.0 copy-start.1
  275.6 4.7 %multiply_convert_fusion = (bf16[1024,512]{1,0:T(8,128)(2,1)}, bf16[1024,512]{1,0:T(8,128)(2,1)}) fusion(bf16[1024,512]{1,0:T(8,128)(2,1)} %param.11, bf16[1024,512]{1,0:T(8,128)(2,1)} %collective-permute-done.9, f32[1024,512]{1,0:T(8,128)} %gather_fusion.7, f32[1024,512]{1,0:T(8,128)} %collective-permute-done.8, pred[1024]{0:T(1024)(128)(4,1)S(1)} %dynamic-slice-done, ...), kind=kLoop, calls=%fused_computation.24 | loop fusion | flops 9961472 | bytes 9438208 | tf_op jit(solution)/shard_map/convert_element_type | solution.py:117
  280.3 0.0 copy-done.1
  (23 shorter events, 0.2 us)
Async XLA Ops:
  0.6 212.5 %copy-start = (bf16[512,2048]{1,0:T(8,128)(2,1)S(1)}, bf16[512,2048]{1,0:T(8,128)(2,1)}, u32[]{:S(2)}) copy-start(bf16[512,2048]{1,0:T(8,128)(2,1)} %param.13) | copy-start | bytes 6291460
  0.6 4.2 %copy-start.2 = (bf16[144,2048]{1,0:T(8,128)(2,1)S(1)}, bf16[144,2048]{1,0:T(8,128)(2,1)}, u32[]{:S(2)}) copy-start(bf16[144,2048]{1,0:T(8,128)(2,1)} %param.7) | copy-start | bytes 1769476
  12.2 200.9 %all-to-all-start = ((bf16[32,80,2048]{2,1,0:T(8,128)(2,1)}), bf16[32,80,2048]{2,1,0:T(8,128)(2,1)}, u32[]{:S(2)}, u32[]{:S(2)}) async-start(bf16[32,80,2048]{2,1,0:T(8,128)(2,1)} %stack.8), calls=%async_computation | async-start | bytes 20971520 | tf_op jit(solution)/shard_map/all_to_all | solution.py:14
  23.5 3.0 %copy-start.5 = (s32[1,32]{1,0:T(1,128)S(1)}, s32[1,32]{1,0:T(1,128)}, u32[]{:S(2)}) copy-start(s32[1,32]{1,0:T(1,128)} %param.10) | copy-start | bytes 388
  25.7 126.3 %collective-permute-start = (bf16[1024,512]{1,0:T(8,128)(2,1)S(1)}, bf16[1024,512]{1,0:T(8,128)(2,1)}, u32[]{:S(2)}, u32[]{:S(2)}) collective-permute-start(bf16[1024,512]{1,0:T(8,128)(2,1)S(1)} %fusion), channel_id=1, source_target_pairs={{0,2},{1,3},{2,0},{3,1},{4,6},{5,7},{6,4},{7,5},{8,10},{9,11},{10,... | collective-permute-start | bytes 3145736 | tf_op jit(solution)/shard_map/ppermute | solution.py:30
  26.5 93.7 %collective-permute-start.2 = (s32[1,32]{1,0:T(1,128)S(1)}, s32[1,32]{1,0:T(1,128)S(1)}, u32[]{:S(2)}, u32[]{:S(2)}) collective-permute-start(s32[1,32]{1,0:T(1,128)S(1)} %copy-done.5), channel_id=1, source_target_pairs={{0,4},{4,0},{8,12},{12,8},{16,20},{20,16},{24,28},{28,24},{32,36},... | collective-permute-start | bytes 392 | tf_op jit(solution)/shard_map/ppermute | solution.py:47
  120.3 18.4 %collective-permute-start.3 = (s32[2,32]{1,0:T(2,128)S(1)}, s32[2,32]{1,0:T(2,128)S(1)}, u32[]{:S(2)}, u32[]{:S(2)}) collective-permute-start(s32[2,32]{1,0:T(2,128)S(1)} %add_select_fusion.5), channel_id=1, source_target_pairs={{0,8},{4,12},{8,0},{12,4},{16,24},{20,28},{24,16},{28,20},{32,40},... | collective-permute-start | bytes 776 | tf_op jit(solution)/shard_map/ppermute | solution.py:47
  138.7 36.1 %collective-permute-start.4 = (s32[4,32]{1,0:T(4,128)S(1)}, s32[4,32]{1,0:T(4,128)S(1)}, u32[]{:S(2)}, u32[]{:S(2)}) collective-permute-start(s32[4,32]{1,0:T(4,128)S(1)} %add_select_fusion.4), channel_id=1, source_target_pairs={{0,16},{4,20},{8,24},{12,28},{16,0},{20,4},{24,8},{28,12},{32,48},... | collective-permute-start | bytes 1544 | tf_op jit(solution)/shard_map/ppermute | solution.py:47
  154.7 38.7 %collective-permute-start.1 = (bf16[2,1024,512]{2,1,0:T(8,128)(2,1)}, bf16[2,1024,512]{2,1,0:T(8,128)(2,1)}, u32[]{:S(2)}, u32[]{:S(2)}) collective-permute-start(bf16[2,1024,512]{2,1,0:T(8,128)(2,1)} %pad_maximum_fusion.1), channel_id=1, source_target_pairs={{0,1},{1,0},{2,3},{3,2},{4,5},{5,4},{6,7},{7,6},{8,9},{9,8},{10,11... | collective-permute-start | bytes 6291464 | tf_op jit(solution)/shard_map/ppermute | solution.py:32
  174.8 10.8 %collective-permute-start.5 = (s32[8,32]{1,0:T(8,128)S(1)}, s32[8,32]{1,0:T(8,128)S(1)}, u32[]{:S(2)}, u32[]{:S(2)}) collective-permute-start(s32[8,32]{1,0:T(8,128)S(1)} %add_select_fusion.3), channel_id=1, source_target_pairs={{0,32},{4,36},{8,40},{12,44},{16,48},{20,52},{24,56},{28,60},{32,0... | collective-permute-start | bytes 3080 | tf_op jit(solution)/shard_map/ppermute | solution.py:47
  185.6 4.0 %collective-permute-start.6 = (s32[16,32]{1,0:T(8,128)S(1)}, s32[16,32]{1,0:T(8,128)S(1)}, u32[]{:S(2)}, u32[]{:S(2)}) collective-permute-start(s32[16,32]{1,0:T(8,128)S(1)} %add_select_fusion.2), channel_id=1, source_target_pairs={{0,64},{4,68},{8,72},{12,76},{16,80},{20,84},{24,88},{28,92},{32,9... | collective-permute-start | bytes 6152 | tf_op jit(solution)/shard_map/ppermute | solution.py:47
  190.9 59.9 %copy-start.4 = (pred[4096]{0:T(1024)(128)(4,1)}, pred[4096]{0:T(1024)(128)(4,1)S(1)}, u32[]{:S(2)}) copy-start(pred[4096]{0:T(1024)(128)(4,1)S(1)} %lt.92) | copy-start | bytes 12292
  230.7 10.6 %collective-permute-start.7 = (f32[1024,512]{1,0:T(8,128)}, f32[1024,512]{1,0:T(8,128)}, u32[]{:S(2)}, u32[]{:S(2)}) collective-permute-start(f32[1024,512]{1,0:T(8,128)} %gather_fusion.6), channel_id=1, source_target_pairs={{0,1},{1,0},{2,3},{3,2},{4,5},{5,4},{6,7},{7,6},{8,9},{9,8},{10,11... | collective-permute-start | bytes 6291464 | tf_op jit(solution)/shard_map/ppermute | solution.py:103
  250.7 24.8 %collective-permute-start.8 = (f32[1024,512]{1,0:T(8,128)S(1)}, f32[1024,512]{1,0:T(8,128)}, u32[]{:S(2)}, u32[]{:S(2)}) collective-permute-start(f32[1024,512]{1,0:T(8,128)S(1)} %gather_fusion.8), channel_id=1, source_target_pairs={{0,1},{1,0},{2,3},{3,2},{4,5},{5,4},{6,7},{7,6},{8,9},{9,8},{10,11... | collective-permute-start | bytes 6291464 | tf_op jit(solution)/shard_map/ppermute | solution.py:107
  250.8 24.7 %collective-permute-start.9 = (bf16[1024,512]{1,0:T(8,128)(2,1)}, bf16[1024,512]{1,0:T(8,128)(2,1)}, u32[]{:S(2)}, u32[]{:S(2)}) collective-permute-start(bf16[1024,512]{1,0:T(8,128)(2,1)} %add_convert_fusion), channel_id=1, source_target_pairs={{0,2},{1,3},{2,0},{3,1},{4,6},{5,7},{6,4},{7,5},{8,10},{9,11},{10,... | collective-permute-start | bytes 3145736 | tf_op jit(solution)/shard_map/ppermute | solution.py:106
  262.1 13.5 %copy-start.3 = (bf16[1024,512]{1,0:T(8,128)(2,1)S(1)}, bf16[1024,512]{1,0:T(8,128)(2,1)}, u32[]{:S(2)}) copy-start(bf16[1024,512]{1,0:T(8,128)(2,1)} %param.12) | copy-start | bytes 3145732
  262.1 13.5 %dynamic-slice-start = ((pred[4096]{0:T(1024)(128)(4,1)}, s32[]{:T(128)}), pred[1024]{0:T(1024)(128)(4,1)S(1)}, s32[]{:S(2)}) async-start(pred[4096]{0:T(1024)(128)(4,1)} %copy-done.4, s32[]{:T(128)} %select_n.172), calls=%async_computation.1 | async-start | bytes 2560 | tf_op jit(solution)/shard_map/dynamic_slice | solution.py:114
  275.6 4.8 %copy-start.1 = (bf16[512,2048]{1,0:T(8,128)(2,1)S(1)}, bf16[512,2048]{1,0:T(8,128)(2,1)}, u32[]{:S(2)}) copy-start(bf16[512,2048]{1,0:T(8,128)(2,1)} %param.13) | copy-start | bytes 6291460
